TPU v7x, 32 devices: a whole 2x2x4 slice. The times are simulated.
32 devices in a mesh: seq: 8 (over z, x), tp: 4 (over y, core).
Axes of the slice: x: 2, y: 2, z: 4, core: 2. Of those that a mesh axis runs over, the one named last changes fastest.
Arguments:
- hidden: bfloat16 [2048, 2048], P('seq', 'tp'), may hold values from -40 to 40
- new_queries: bfloat16 [2048, 2048], P('seq', 'tp'), may hold values from -9 to 9
- new_keys: bfloat16 [2048, 2048], P('seq', 'tp'), may hold values from -6 to 6
- new_values: bfloat16 [2048, 2048], P('seq', 'tp'), may hold values from -6 to 6
- cache_keys: bfloat16 [8, 4096, 2048], P('seq', None, 'tp'), may hold values from -6 to 6
- cache_values: bfloat16 [8, 4096, 2048], P('seq', None, 'tp'), may hold values from -6 to 6
- cache_lengths: int32 [8], replicated, may hold values from 1 to 4096, as said below
- out_proj: bfloat16 [2048, 2048], P('tp'), may hold values from -0.5 to 0.5
- moe_gain: float32 [2048], P('tp'), may hold values from 0.1 to 1.9
- expert_ids: int32 [2048, 8], P('seq'), may hold values from 0 to 15, all different within a row; in each aligned block of 256 rows (0 to 255, 256 to 511, ...) at most 192 rows name the same one
- route_weights: float32 [2048, 8], P('seq'), may hold values from 0.25 to 0.5
- expert_gate_up: bfloat16 [16, 2048, 2, 1024], P('seq', None, None, 'tp'), may hold values from -0.125 to 0.125
- expert_down: bfloat16 [16, 1024, 2048], P('seq', 'tp'), may hold values from -0.375 to 0.375
- next_gain: float32 [2048], P('tp'), may hold values from 0.1 to 1.9
- qkv_proj: bfloat16 [2048, 3, 2048], P(None, None, 'tp'), may hold values from -0.125 to 0.125
- query_gain: float32 [2048], P('tp'), may hold values from 0.1 to 1.9
- key_gain: float32 [2048], P('tp'), may hold values from 0.1 to 1.9
Outputs:
- layer_out: bfloat16 [2048, 2048], P('seq', 'tp')
- next_query: bfloat16 [2048, 2048], P('seq', 'tp')
- next_key: bfloat16 [2048, 2048], P('seq', 'tp')
- next_value: bfloat16 [2048, 2048], P('seq', 'tp')
Inputs may be any that keep to these rules, and one draw needn't show every extreme that they name: Request r has cached positions 0 to cache_lengths[r] - 1; one request has 4096 of them and one has 1. `expert_ids`: each row names 8 different experts; among the 256 rows of one request no expert is named more than 192 times, and in some request one expert is named exactly 192 times.
All inputs are finite; a program needn't handle non-finite values.
Results may differ from a plain program's by a relative error of at most 0.017.
Values may be sent and summed in bfloat16 or wider, within the bound.
No kernel may reach another device: no remote copies, remote signals or barrier semaphores. Data moves between devices by JAX's collectives and lax.ppermute only.
A program may use at most 128 MiB of HBM per device.

v0:
```python
import math
import jax
import jax.numpy as jnp
from jax import lax
from jax.sharding import PartitionSpec as P

D = 2048
HEAD_DIM = 128
TOP = 8
NEW = 256
epsilon = 1e-05


def softmax_parts(queries, key_rows, values, allowed):
    scores = jnp.einsum(
        "bthe,bche->bhtc", queries, key_rows, preferred_element_type=jnp.float32
    ) / math.sqrt(HEAD_DIM)
    scores = jnp.where(allowed[:, None], scores, -1e30)
    row_max = jnp.max(scores, axis=3)
    weights = jnp.where(allowed[:, None], jnp.exp(scores - row_max[..., None]), 0.0)
    row_total = jnp.sum(weights, axis=3)
    partial_out = jnp.einsum(
        "bhtc,bche->bthe", weights.astype(jnp.bfloat16), values, preferred_element_type=jnp.float32
    )
    return (partial_out, jnp.swapaxes(row_max, 1, 2), jnp.swapaxes(row_total, 1, 2))


def combine_parts(first, second):
    out_a, max_a, total_a = first
    out_b, max_b, total_b = second
    joint = jnp.maximum(max_a, max_b)
    factor_a = jnp.exp(max_a - joint)
    factor_b = jnp.exp(max_b - joint)
    return (
        out_a * factor_a[..., None] + out_b * factor_b[..., None],
        joint,
        total_a * factor_a + total_b * factor_b,
    )


def merge_parts(pieces, maxima, totals):
    overall = jnp.max(maxima, axis=0)
    factor = jnp.exp(maxima - overall[None])
    denominator = jnp.sum(totals * factor, axis=0)
    merged = jnp.sum(pieces * factor[..., None], axis=0)
    return merged / denominator[..., None]


def dense_experts(moe_in, expert_ids, route_weights, expert_gate_up, down_full, here, experts_all):
    local_experts = expert_gate_up.shape[0]
    hidden_quarter = expert_gate_up.shape[3]
    tokens, quarter = moe_in.shape
    seq_count = experts_all // local_experts
    gate_w = jnp.sum(
        route_weights[:, :, None]
        * (expert_ids[:, :, None] == jnp.arange(experts_all, dtype=jnp.int32)[None, None, :]),
        axis=1,
    )
    gate_t = jnp.transpose(gate_w)
    gate_hi = gate_t.astype(jnp.bfloat16)
    gate_lo = (gate_t - gate_hi.astype(jnp.float32)).astype(jnp.bfloat16)
    info = jnp.concatenate([gate_hi, gate_lo], axis=0).reshape(-1, quarter)
    packed = jnp.concatenate([moe_in, info], axis=0)
    gathered = lax.all_gather(packed, "seq", axis=0, tiled=False)
    rows_q = gathered[:, :tokens].reshape(seq_count * tokens, quarter)
    info_all = gathered[:, tokens:].reshape(seq_count, 2, experts_all, tokens).astype(jnp.float32)
    gate_all = info_all[:, 0] + info_all[:, 1]
    gate_local = lax.dynamic_slice_in_dim(gate_all, here * local_experts, local_experts, axis=1)
    gate_local = jnp.transpose(gate_local, (1, 0, 2)).reshape(local_experts, seq_count * tokens)
    rows = lax.all_gather(rows_q, "tp", axis=1, tiled=True)
    gate_up = expert_gate_up.reshape(local_experts, D, 2 * hidden_quarter)
    projected = jnp.einsum("td,edf->etf", rows, gate_up, preferred_element_type=jnp.float32)
    activated = jax.nn.silu(projected[..., :hidden_quarter]) * projected[..., hidden_quarter:]
    activated = activated.astype(jnp.bfloat16).astype(jnp.float32)
    weighted = (activated * gate_local[:, :, None]).astype(jnp.bfloat16)
    weighted = lax.all_gather(weighted, "tp", axis=2, tiled=True)
    partial = jnp.einsum(
        "etf,efd->td", weighted, down_full, preferred_element_type=jnp.float32
    ).astype(jnp.bfloat16)
    partial = lax.psum_scatter(partial, "seq", scatter_dimension=0, tiled=True)
    return partial.astype(jnp.float32)


def dispatch_experts(
    moe_in, expert_ids, route_weights, expert_gate_up, expert_down, experts_all, capacity
):
    quarter = moe_in.shape[1]
    local_experts = expert_gate_up.shape[0]
    flat_ids = expert_ids.reshape(NEW * TOP)
    onehot = (flat_ids[:, None] == jnp.arange(experts_all, dtype=jnp.int32)[None, :]).astype(
        jnp.int32
    )
    ranks = jnp.sum((jnp.cumsum(onehot, axis=0) - onehot) * onehot, axis=1)
    target = (flat_ids * capacity + ranks).reshape(NEW, TOP)
    slot_ids = jnp.arange(experts_all * capacity, dtype=jnp.int32)
    selector = jnp.sum(
        (target[None, :, :] == slot_ids[:, None, None]).astype(jnp.int32), axis=2
    ).astype(jnp.bfloat16)
    send_rows = jnp.dot(selector, moe_in, preferred_element_type=jnp.float32).astype(jnp.bfloat16)
    send_rows = send_rows.reshape(experts_all, capacity, quarter)
    received = lax.all_to_all(send_rows, "seq", split_axis=0, concat_axis=1, tiled=True)
    hidden_quarter = expert_gate_up.shape[3]
    gate_up_local = expert_gate_up.reshape(local_experts, D, 2 * hidden_quarter)
    weight_rows = gate_up_local
    projected = jnp.einsum(
        "erd,edf->erf",
        lax.all_gather(received, "tp", axis=2, tiled=True),
        weight_rows,
        preferred_element_type=jnp.float32,
    )
    activated = (
        jax.nn.silu(projected[..., :hidden_quarter]) * projected[..., hidden_quarter:]
    ).astype(jnp.bfloat16)
    down_terms = jnp.einsum(
        "erf,efd->erd", activated, expert_down, preferred_element_type=jnp.float32
    )
    expert_result = lax.psum_scatter(
        down_terms.astype(jnp.bfloat16), "tp", scatter_dimension=2, tiled=True
    )
    returned = lax.all_to_all(
        expert_result, "seq", split_axis=1, concat_axis=0, tiled=True
    ).reshape(experts_all * capacity, quarter)
    picked = jnp.take(returned, target, axis=0)
    return jnp.sum(route_weights[:, :, None] * picked.astype(jnp.float32), axis=1)


def body(
    hidden,
    new_queries,
    new_keys,
    new_values,
    cache_keys,
    cache_values,
    cache_lengths,
    out_proj,
    moe_gain,
    expert_ids,
    route_weights,
    expert_gate_up,
    expert_down,
    next_gain,
    qkv_proj,
    query_gain,
    key_gain,
):
    seq_count = lax.axis_size("seq")
    here = lax.axis_index("seq")
    local_experts = expert_gate_up.shape[0]
    experts_all = local_experts * seq_count
    capacity = max(2, 3 * NEW * TOP // (2 * experts_all))
    dense = NEW <= 2 * capacity
    if dense:
        tp_here = lax.axis_index("tp")
        quarter_width = hidden.shape[1]
        down_full = lax.all_gather(expert_down, "tp", axis=1, tiled=True)
        down_full = lax.dynamic_slice_in_dim(
            down_full, tp_here * quarter_width, quarter_width, axis=2
        )
    local_width = new_queries.shape[1]
    local_heads = local_width // HEAD_DIM
    quarter = hidden.shape[1]
    own_queries = new_queries.reshape(1, NEW, local_heads, HEAD_DIM)
    own_keys = new_keys.reshape(1, NEW, local_heads, HEAD_DIM)
    own_values = new_values.reshape(1, NEW, local_heads, HEAD_DIM)
    offsets = jnp.arange(NEW, dtype=jnp.int32)
    causal = (offsets[None, :] <= offsets[:, None])[None]
    own_out, own_max, own_total = softmax_parts(own_queries, own_keys, own_values, causal)
    span = cache_keys.shape[1]
    block = min(512, span)
    my_length = lax.dynamic_index_in_dim(cache_lengths, here, 0, keepdims=False)
    block_count = (my_length + block - 1) // block
    key_blocks = cache_keys.reshape(span, local_heads, HEAD_DIM)
    value_blocks = cache_values.reshape(span, local_heads, HEAD_DIM)

    def cache_block(index, carry):
        begin = index * block
        keys_here = lax.dynamic_slice_in_dim(key_blocks, begin, block, 0)[None]
        values_here = lax.dynamic_slice_in_dim(value_blocks, begin, block, 0)[None]
        positions = begin + jnp.arange(block, dtype=jnp.int32)
        allowed = jnp.broadcast_to((positions < my_length)[None, None, :], (1, NEW, block))
        return combine_parts(carry, softmax_parts(own_queries, keys_here, values_here, allowed))

    start_parts = (
        jnp.zeros((1, NEW, local_heads, HEAD_DIM), jnp.float32),
        jnp.full((1, NEW, local_heads), -1e30, jnp.float32),
        jnp.zeros((1, NEW, local_heads), jnp.float32),
    )
    pieces, maxima, totals = lax.fori_loop(0, block_count, cache_block, start_parts)
    attended = merge_parts(
        jnp.concatenate([own_out, pieces], 0),
        jnp.concatenate([own_max, maxima], 0),
        jnp.concatenate([own_total, totals], 0),
    )
    attended = attended.reshape(NEW, local_width).astype(jnp.bfloat16)
    if dense:
        attended, down_full = lax.optimization_barrier((attended, down_full))
    attn_term = jnp.dot(attended, out_proj, preferred_element_type=jnp.float32)
    residual = hidden.astype(jnp.float32) + lax.psum_scatter(
        attn_term.astype(jnp.bfloat16), "tp", scatter_dimension=1, tiled=True
    ).astype(jnp.float32)
    square_total = lax.psum(jnp.sum(residual * residual, axis=1), "tp")
    moe_in = (residual * lax.rsqrt(square_total / D + epsilon)[:, None] * moe_gain[None, :]).astype(
        jnp.bfloat16
    )
    if dense:
        moe_term = dense_experts(
            moe_in, expert_ids, route_weights, expert_gate_up, down_full, here, experts_all
        )
    else:
        moe_term = dispatch_experts(
            moe_in, expert_ids, route_weights, expert_gate_up, expert_down, experts_all, capacity
        )
    routed = residual + moe_term
    layer_out = routed.astype(jnp.bfloat16)
    scaled = (routed * next_gain[None, :]).astype(jnp.bfloat16)
    qkv_local = qkv_proj.reshape(D, 3 * local_width)
    weight_rows = qkv_local
    mixed = jnp.dot(
        lax.all_gather(scaled, "tp", axis=1, tiled=True),
        weight_rows,
        preferred_element_type=jnp.float32,
    )
    mixed = mixed.reshape(NEW, 3, local_width)
    squares_routed = jnp.sum(routed * routed, axis=1)
    routed_total, query_raw, key_raw = lax.psum(
        (
            squares_routed,
            jnp.sum(mixed[:, 0] * mixed[:, 0], axis=1),
            jnp.sum(mixed[:, 1] * mixed[:, 1], axis=1),
        ),
        "tp",
    )
    x_scale = lax.rsqrt(routed_total / D + epsilon)
    query_pre = mixed[:, 0] * x_scale[:, None]
    key_pre = mixed[:, 1] * x_scale[:, None]
    query_total = query_raw * x_scale * x_scale
    key_total = key_raw * x_scale * x_scale
    next_query = (
        query_pre * lax.rsqrt(query_total / D + epsilon)[:, None] * query_gain[None, :]
    ).astype(jnp.bfloat16)
    next_key = (key_pre * lax.rsqrt(key_total / D + epsilon)[:, None] * key_gain[None, :]).astype(
        jnp.bfloat16
    )
    next_value = (mixed[:, 2] * x_scale[:, None]).astype(jnp.bfloat16)
    return (layer_out, next_query, next_key, next_value)


def solution(mesh):
    return jax.shard_map(
        body,
        mesh=mesh,
        in_specs=(
            P("seq", "tp"),
            P("seq", "tp"),
            P("seq", "tp"),
            P("seq", "tp"),
            P("seq", None, "tp"),
            P("seq", None, "tp"),
            P(),
            P("tp", None),
            P("tp"),
            P("seq", None),
            P("seq", None),
            P("seq", None, None, "tp"),
            P("seq", "tp", None),
            P("tp"),
            P(None, None, "tp"),
            P("tp"),
            P("tp"),
        ),
        out_specs=(P("seq", "tp"), P("seq", "tp"), P("seq", "tp"), P("seq", "tp")),
        check_vma=False,
    )
```

profile of v0, /device:TPU:0, one launch (start us, length us, event | category | flops | bytes accessed | tf_op | source)
XLA Modules:
  0.0 412.0 jit_solution(3361592434585957795)
XLA Ops:
  9.6 6.4 %copy.95 = bf16[1,4096,512]{1,2,0:T(8,128)(2,1)} copy(bf16[1,4096,512]{2,1,0:T(8,128)(2,1)} %param.23) | data formatting | bytes 8388608 | tf_op args[4]
  16.0 6.6 %copy.97 = bf16[1,4096,512]{1,2,0:T(8,128)(2,1)} copy(bf16[1,4096,512]{2,1,0:T(8,128)(2,1)} %param.24) | data formatting | bytes 8388608 | tf_op args[5]
  22.7 28.9 %while.14 = (s32[]{:T(128)}, f32[1,256,4,128]{1,3,2,0:T(8,128)S(1)}, f32[1,256,4]{1,2,0:T(4,128)S(1)}, f32[1,256,4]{1,2,0:T(4,128)S(1)}, s32[]{:T(128)}, /*index...) while((s32[]{:T(128)}, ...), condition=%wide.region_4.5_spmd, body=%wide.region_1.4_spmd.sunk | while | flops 275651584 | bytes 8731323 | solution.py:188
  25.7 1.8 fusion.83
  40.1 1.8 fusion.83
  54.5 16.1 %all-gather.7.cloned.1.call-done = bf16[2,1024,2048]{2,1,0:T(8,128)(2,1)} async-done(((bf16[2,256,2048]{2,1,0:T(8,128)(2,1)}), bf16[2,1024,2048]{2,1,0:T(8,128)(2,1)}) %all-gather.7.cloned.1.call-update) | async-done | bytes 8388624 | tf_op jit(solution)/shard_map/all_gather | solution.py:155
  70.6 3.0 constant_dynamic-slice_fusion
  75.5 24.9 %reduce-scatter.3.cloned.1.call-done = bf16[256,512]{1,0:T(8,128)(2,1)} async-done(((bf16[256,2048]{1,0:T(8,128)(2,1)}), bf16[256,512]{1,0:T(8,128)(2,1)}) %reduce-scatter.3.cloned.1.call-update) | async-done | bytes 262160 | tf_op jit(solution)/shard_map/reduce_scatter | solution.py:198
  101.6 5.8 %psum.28 = f32[256]{0:T(256)S(1)} all-reduce(f32[256]{0:T(256)S(1)} %multiply_reduce_fusion.3), channel_id=1, replica_groups=mesh['seq'=8,'tp'=4] {'tp'}, use_global_device_ids=true, to_apply=%region_10.11 | all-reduce | flops 256 | bytes 2048 | tf_op jit(solution)/shard_map/psum | solution.py:201
  109.2 51.9 %all-gather.15.cloned.1.call-done = bf16[2176,512]{1,0:T(8,128)(2,1)} async-done(((bf16[272,512]{1,0:T(8,128)(2,1)}), bf16[2176,512]{1,0:T(8,128)(2,1)}) %all-gather.15.cloned.1.call-update) | async-done | bytes 2228240 | tf_op jit(solution)/shard_map/all_gather | solution.py:64
  161.1 3.1 slice.40
  164.2 7.8 %reshape.166 = bf16[2,2048,512]{2,1,0:T(8,128)(2,1)} reshape(bf16[2,2048,2,256]{3,2,1,0:T(2,128)(2,1)} %param.30) | data formatting | bytes 8388608 | tf_op jit(solution)/shard_map/reshape | solution.py:71
  173.1 48.0 %all-gather.9.cloned.1.call-done = bf16[2048,2048]{1,0:T(8,128)(2,1)} async-done(((bf16[2048,512]{1,0:T(8,128)(2,1)}), bf16[2048,2048]{1,0:T(8,128)(2,1)}) %all-gather.9.cloned.1.call-update) | async-done | bytes 8388624 | tf_op jit(solution)/shard_map/all_gather | solution.py:70
  221.1 12.4 %fusion.29 = f32[2,2048,512]{2,1,0:T(8,128)S(1)} fusion(bf16[2,2048,512]{2,1,0:T(8,128)(2,1)} %reshape.166, bf16[2048,2048]{1,0:T(8,128)(2,1)} %all-gather.9.cloned.1.call-done), kind=kOutput, calls=%fused_computation.37 | convolution fusion | flops 8589934592 | bytes 20971520 | tf_op jit(solution)/shard_map/td,edf->etf/dot_general | solution.py:72
  233.6 2.2 multiply_convert_fusion
  236.0 59.3 %all-gather.11.cloned.1.call-done = bf16[2,2048,1024]{2,1,0:T(8,128)(2,1)} async-done(((bf16[2,2048,256]{2,1,0:T(8,128)(2,1)}), bf16[2,2048,1024]{2,1,0:T(8,128)(2,1)}) %all-gather.11.cloned.1.call-update) | async-done | bytes 8388624 | tf_op jit(solution)/shard_map/all_gather | solution.py:76
  295.3 9.1 %bitcast_convert_fusion = bf16[2048,512]{1,0:T(8,128)(2,1)} fusion(bf16[2,2048,1024]{2,1,0:T(8,128)(2,1)} %all-gather.11.cloned.1.call-done, bf16[2,1024,512]{2,1,0:T(8,128)(2,1)S(1)} %copy-done.5), kind=kOutput, calls=%fused_computation.40 | convolution fusion | flops 4296015872 | bytes 12582912 | tf_op jit(solution)/shard_map/etf,efd->td/dot_general | solution.py:77
  304.5 68.0 %reduce-scatter.5.cloned.1.call-done = bf16[256,512]{1,0:T(8,128)(2,1)} async-done(((bf16[2048,512]{1,0:T(8,128)(2,1)}), bf16[256,512]{1,0:T(8,128)(2,1)}) %reduce-scatter.5.cloned.1.call-update) | async-done | bytes 262160 | tf_op jit(solution)/shard_map/reduce_scatter | solution.py:80
  372.5 1.9 multiply_reduce_fusion.2
  374.4 8.9 %copy.103 = bf16[2048,3,512]{0,2,1:T(8,128)(2,1)} copy(bf16[2048,3,512]{2,0,1:T(8,128)(2,1)} %param.33) | data formatting | bytes 12582912 | tf_op args[14]
  383.3 7.1 %all-gather.13.cloned.1.call-done = bf16[256,2048]{1,0:T(8,128)(2,1)} async-done(((bf16[256,512]{1,0:T(8,128)(2,1)}), bf16[256,2048]{1,0:T(8,128)(2,1)}) %all-gather.13.cloned.1.call-update) | async-done | bytes 1048592 | tf_op jit(solution)/shard_map/all_gather | solution.py:219
  390.4 5.1 %fusion.27 = f32[256,3,512]{2,0,1:T(8,128)S(1)} fusion(bf16[2048,3,512]{0,2,1:T(8,128)(2,1)} %copy.103, bf16[256,2048]{1,0:T(8,128)(2,1)} %all-gather.13.cloned.1.call-done), kind=kOutput, calls=%fused_computation.35 | convolution fusion | flops 1610612736 | bytes 8912896 | tf_op jit(solution)/shard_map/dot_general | solution.py:218
  396.8 5.9 %all-reduce = (f32[256]{0:T(256)S(1)}, f32[256]{0:T(256)S(1)}, f32[256]{0:T(256)S(1)}) all-reduce(f32[256]{0:T(256)S(1)} %get-tuple-element.107, f32[256]{0:T(256)S(1)} %get-tuple-element.142, f32[256]{0:T(256)S(1)} %get-tuple-element.106), channel_id=1, replica_groups=mesh['seq'=8,'tp'=4] {'tp'}, use_global_device_ids=true, to_apply=%region_16.17 | all-reduce | flops 768 | bytes 6144 | tf_op jit(solution)/shard_map/psum | solution.py:225
  402.7 2.4 fusion.40
  (117 shorter events, 37.0 us)
Async XLA Ops:
  7.2 66.5 %copy-start = (bf16[512,2048]{1,0:T(8,128)(2,1)S(1)}, bf16[512,2048]{1,0:T(8,128)(2,1)}, u32[]{:S(2)}) copy-start(bf16[512,2048]{1,0:T(8,128)(2,1)} %param.26) | copy-start | bytes 6291460
  7.2 0.8 copy-start.14
  7.2 2.1 copy-start.6
  7.2 63.4 %all-gather.7.cloned.1.call-start = ((), (), s32[]{:S(2)}) async-start(), calls=%async_computation.2 | async-start | bytes 10485760 | tf_op jit(solution)/shard_map/all_gather | solution.py:155
  7.9 92.5 %reduce-scatter.3.cloned.1.call-start = ((), (), s32[]{:S(2)}) async-start(), calls=%async_computation.3 | async-start | bytes 1310720 | tf_op jit(solution)/shard_map/reduce_scatter | solution.py:198
  51.8 1.6 copy-start.7
  73.6 1.8 copy-start.8
  73.6 1.8 copy-start.9
  73.6 26.8 %copy-start.3 = (bf16[256,512]{1,0:T(8,128)(2,1)S(1)}, bf16[256,512]{1,0:T(8,128)(2,1)}, u32[]{:S(2)}) copy-start(bf16[256,512]{1,0:T(8,128)(2,1)} %param.19) | copy-start | bytes 786436
  73.7 33.7 %copy-start.10 = (f32[512]{0:T(512)S(1)}, f32[512]{0:T(512)}, u32[]{:S(2)}) copy-start(f32[512]{0:T(512)} %param.27) | copy-start | bytes 6148
  75.4 85.7 %all-gather.15.cloned.1.call-start = ((), (), s32[]{:S(2)}) async-start(), calls=%async_computation.8 | async-start | bytes 2506752 | tf_op jit(solution)/shard_map/all_gather | solution.py:64
  109.1 111.9 %all-gather.9.cloned.1.call-start = ((), (), s32[]{:S(2)}) async-start(), calls=%async_computation.4 | async-start | bytes 10485760 | tf_op jit(solution)/shard_map/all_gather | solution.py:70
  164.1 131.2 %all-gather.11.cloned.1.call-start = ((), (), s32[]{:S(2)}) async-start(), calls=%async_computation.5 | async-start | bytes 10485760 | tf_op jit(solution)/shard_map/all_gather | solution.py:76
  235.7 59.6 %copy-start.5 = (bf16[2,1024,512]{2,1,0:T(8,128)(2,1)S(1)}, bf16[2,1024,512]{2,1,0:T(8,128)(2,1)}, u32[]{:S(2)}) copy-start(bf16[2,1024,512]{2,1,0:T(8,128)(2,1)} %constant_dynamic-slice_fusion) | copy-start | bytes 6291460
  235.8 136.7 %reduce-scatter.5.cloned.1.call-start = ((), (), s32[]{:S(2)}) async-start(), calls=%async_computation.6 | async-start | bytes 2359296 | tf_op jit(solution)/shard_map/reduce_scatter | solution.py:80
  304.4 68.0 %copy-start.4 = (bf16[256,512]{1,0:T(8,128)(2,1)S(1)}, bf16[256,512]{1,0:T(8,128)(2,1)}, u32[]{:S(2)}) copy-start(bf16[256,512]{1,0:T(8,128)(2,1)} %reduce-scatter.3.cloned.1.call-done) | copy-start | bytes 786436
  304.4 68.0 %copy-start.11 = (f32[512]{0:T(512)S(1)}, f32[512]{0:T(512)}, u32[]{:S(2)}) copy-start(f32[512]{0:T(512)} %param.32) | copy-start | bytes 6148
  304.5 86.0 %all-gather.13.cloned.1.call-start = ((), (), s32[]{:S(2)}) async-start(), calls=%async_computation.7 | async-start | bytes 1310720 | tf_op jit(solution)/shard_map/all_gather | solution.py:219
  383.3 19.4 %copy-start.12 = (f32[512]{0:T(512)S(1)}, f32[512]{0:T(512)}, u32[]{:S(2)}) copy-start(f32[512]{0:T(512)} %param.35) | copy-start | bytes 6148
  383.3 19.4 %copy-start.13 = (f32[512]{0:T(512)S(1)}, f32[512]{0:T(512)}, u32[]{:S(2)}) copy-start(f32[512]{0:T(512)} %param.34) | copy-start | bytes 6148
  390.4 14.7 %copy-start.1 = (bf16[512,2048]{1,0:T(8,128)(2,1)S(1)}, bf16[512,2048]{1,0:T(8,128)(2,1)}, u32[]{:S(2)}) copy-start(bf16[512,2048]{1,0:T(8,128)(2,1)} %param.26) | copy-start | bytes 6291460
  395.5 1.2 copy-start.2
Sparse Core Ops, SparseCore 0:
  9.6 60.9 all-gather.6
  75.5 24.8 reduce-scatter.2
  109.3 51.7 all-gather.14
  164.3 56.7 all-gather.8
  235.9 59.3 all-gather.10
  304.6 67.8 reduce-scatter.4
  374.7 15.6 all-gather.12
where the time goes:
time: 414 us; the launch traced here: 412 us
  waiting for transfers between devices  276 us (67%)
  matrix products  50.8 us (12%)
  local copies, waits for them, and re-layouts  38.4 us (9%)
  other arithmetic  19.2 us (5%)
  between operations  15.1 us (4%)
  blocking collectives  11.7 us (3%)
    reduce_scatter x1, waiting for transfers between devices, dense_experts(): partial = lax.psum_scatter(partial, 'seq', scatter_dimension=0, tiled=True)  68 us
    all_gather x1, waiting for transfers between devices, dense_experts(): weighted = lax.all_gather(weighted, 'tp', axis=2, tiled=True)  59.3 us
    all_gather x1, waiting for transfers between devices, dense_experts(): gathered = lax.all_gather(packed, 'seq', axis=0, tiled=False)  51.9 us
    all_gather x1, waiting for transfers between devices, dense_experts(): rows = lax.all_gather(rows_q, 'tp', axis=1, tiled=True)  48 us
    reduce_scatter x1, waiting for transfers between devices, body(): lax.psum_scatter(attn_term.astype(jnp.bfloat16), 'tp', scatter_dimension=...  24.9 us
    unnamed x35, local copies, waits for them, and re-layouts  23.3 us
    all_gather x1, waiting for transfers between devices, body(): down_full = lax.all_gather(expert_down, 'tp', axis=1, tiled=True)  16.1 us
    dot_general x1, matrix products, dense_experts(): jnp.einsum('td,edf->etf', rows, gate_up, preferred_element_type=jnp.float32)  12.4 us
  transfers between devices with their start and end apart: 7, of which 7 were waited for; matrix products, arithmetic and copies ran while one was open for 15% of the time, Pallas kernels for 0%

commit v1 on v0

--- a/solution.py
+++ b/solution.py
@@ -73,7 +73,19 @@
     activated = jax.nn.silu(projected[..., :hidden_quarter]) * projected[..., hidden_quarter:]
     activated = activated.astype(jnp.bfloat16).astype(jnp.float32)
     weighted = (activated * gate_local[:, :, None]).astype(jnp.bfloat16)
-    weighted = lax.all_gather(weighted, "tp", axis=2, tiled=True)
+    sides = lax.axis_size("tp")
+    runs = tuple(((rr, (rr + 1) % sides) for rr in range(sides)))
+    lanes = tuple(((rr, (rr - 1) % sides) for rr in range(sides)))
+    newest, shaped = ([weighted], [weighted])
+    for _ in range(sides // 2):
+        spare = lax.ppermute(newest[-1], "tp", runs)
+        newest.append(spare)
+    for _ in range((sides - 1) // 2):
+        shaped.append(lax.ppermute(shaped[-1], "tp", perm=lanes))
+    reached = jnp.concatenate([*newest[::-1], *shaped[1:]], axis=2)
+    weighted = jnp.roll(
+        reached, shift=(lax.axis_index("tp") - sides // 2) * weighted.shape[2], axis=2
+    )
     partial = jnp.einsum(
         "etf,efd->td", weighted, down_full, preferred_element_type=jnp.float32
     ).astype(jnp.bfloat16)

time: 414 us -> 440 us (1.063)
  local copies, waits for them, and re-layouts: 38.4 us -> 51.2 us
  other arithmetic: 19.2 us -> 26.3 us
  waiting for transfers between devices: 276 us -> 282 us
    ppermute x0 -> x3, waiting for transfers between devices: none -> 70.9 us  [the longest x2 70.9 us: dense_experts(): spare = lax.ppermute(newest[-1], 'tp', runs)]
    all_gather x1 -> x0, waiting for transfers between devices: 59.3 us -> none  [dense_experts(): weighted = lax.all_gather(weighted, 'tp', axis=2, tiled=True)]
    unnamed x35 -> x42, local copies, waits for them, and re-layouts: 23.3 us -> 29.8 us
    unnamed x0 -> x3, other arithmetic: none -> 6.27 us
  transfers between devices with their start and end apart: 7 -> 9, of which waited for: 7 -> 8; matrix products, arithmetic and copies ran while one was open for 15% -> 17% of each run, Pallas kernels for 0% -> 0%
where the time goes in v1:
time: 440 us; the launch traced here: 438 us
  waiting for transfers between devices  282 us (64%)
  local copies, waits for them, and re-layouts  51.2 us (12%)
  matrix products  48.5 us (11%)
  other arithmetic  26.3 us (6%)
  between operations  15.2 us (3%)
  blocking collectives  11.7 us (3%)
    ppermute x2, waiting for transfers between devices, dense_experts(): spare = lax.ppermute(newest[-1], 'tp', runs)  70.9 us
    reduce_scatter x1, waiting for transfers between devices, dense_experts(): partial = lax.psum_scatter(partial, 'seq', scatter_dimension=0, tiled=True)  67.7 us
    all_gather x1, waiting for transfers between devices, dense_experts(): gathered = lax.all_gather(packed, 'seq', axis=0, tiled=False)  51.9 us
    all_gather x1, waiting for transfers between devices, dense_experts(): rows = lax.all_gather(rows_q, 'tp', axis=1, tiled=True)  44.4 us
    unnamed x42, local copies, waits for them, and re-layouts  29.8 us
    reduce_scatter x1, waiting for transfers between devices, body(): lax.psum_scatter(attn_term.astype(jnp.bfloat16), 'tp', scatter_dimension=...  24.9 us
    all_gather x1, waiting for transfers between devices, body(): down_full = lax.all_gather(expert_down, 'tp', axis=1, tiled=True)  14.6 us
    dot_general x1, matrix products, dense_experts(): jnp.einsum('td,edf->etf', rows, gate_up, preferred_element_type=jnp.float32)  12.5 us
  transfers between devices with their start and end apart: 9, of which 8 were waited for; matrix products, arithmetic and copies ran while one was open for 17% of the time, Pallas kernels for 0%

profile of v1, /device:TPU:0, one launch (start us, length us, event | category | flops | bytes accessed | tf_op | source)
XLA Modules:
  0.0 437.6 jit_solution(8751061556165997770)
XLA Ops:
  9.9 6.4 %copy.105 = bf16[1,4096,512]{1,2,0:T(8,128)(2,1)} copy(bf16[1,4096,512]{2,1,0:T(8,128)(2,1)} %param.23) | data formatting | bytes 8388608 | tf_op args[4]
  16.6 6.5 %copy.107 = bf16[1,4096,512]{1,2,0:T(8,128)(2,1)} copy(bf16[1,4096,512]{2,1,0:T(8,128)(2,1)} %param.24) | data formatting | bytes 8388608 | tf_op args[5]
  23.2 28.9 %while.14 = (s32[]{:T(128)}, f32[1,256,4,128]{1,3,2,0:T(8,128)S(1)}, f32[1,256,4]{1,2,0:T(4,128)S(1)}, f32[1,256,4]{1,2,0:T(4,128)S(1)}, s32[]{:T(128)}, /*index...) while((s32[]{:T(128)}, ...), condition=%wide.region_4.5_spmd, body=%wide.region_1.4_spmd.sunk | while | flops 275651584 | bytes 8731331 | solution.py:200
  56.0 14.6 %all-gather.6.cloned.1.call-done = bf16[2,1024,2048]{2,1,0:T(8,128)(2,1)} async-done(((bf16[2,256,2048]{2,1,0:T(8,128)(2,1)}), bf16[2,1024,2048]{2,1,0:T(8,128)(2,1)}) %all-gather.6.cloned.1.call-update) | async-done | bytes 8388624 | tf_op jit(solution)/shard_map/all_gather | solution.py:167
  70.6 3.0 constant_dynamic-slice_fusion
  75.5 24.9 %reduce-scatter.3.cloned.1.call-done = bf16[256,512]{1,0:T(8,128)(2,1)} async-done(((bf16[256,2048]{1,0:T(8,128)(2,1)}), bf16[256,512]{1,0:T(8,128)(2,1)}) %reduce-scatter.3.cloned.1.call-update) | async-done | bytes 262160 | tf_op jit(solution)/shard_map/reduce_scatter | solution.py:210
  101.5 5.8 %psum.28 = f32[256]{0:T(256)S(1)} all-reduce(f32[256]{0:T(256)S(1)} %multiply_reduce_fusion.3), channel_id=1, replica_groups=mesh['seq'=8,'tp'=4] {'tp'}, use_global_device_ids=true, to_apply=%region_10.11 | all-reduce | flops 256 | bytes 2048 | tf_op jit(solution)/shard_map/psum | solution.py:213
  109.1 51.9 %all-gather.12.cloned.1.call-done = bf16[2176,512]{1,0:T(8,128)(2,1)} async-done(((bf16[272,512]{1,0:T(8,128)(2,1)}), bf16[2176,512]{1,0:T(8,128)(2,1)}) %all-gather.12.cloned.1.call-update) | async-done | bytes 2228240 | tf_op jit(solution)/shard_map/all_gather | solution.py:64
  161.0 3.1 slice.40
  164.1 11.5 %copy.120 = bf16[2,2048,2,256]{1,3,2,0:T(8,128)(2,1)} copy(bf16[2,2048,2,256]{3,2,1,0:T(2,128)(2,1)} %param.30) | data formatting | bytes 8388608 | tf_op jit(solution)/shard_map/reshape | solution.py:71
  176.7 44.4 %all-gather.8.cloned.1.call-done = bf16[2048,2048]{1,0:T(8,128)(2,1)} async-done(((bf16[2048,512]{1,0:T(8,128)(2,1)}), bf16[2048,2048]{1,0:T(8,128)(2,1)}) %all-gather.8.cloned.1.call-update) | async-done | bytes 8388624 | tf_op jit(solution)/shard_map/all_gather | solution.py:70
  221.1 12.5 %fusion.31 = f32[2,2048,512]{1,2,0:T(8,128)S(1)} fusion(bf16[2,2048,512]{1,2,0:T(8,128)(2,1)} %bitcast.168, bf16[2048,2048]{1,0:T(8,128)(2,1)} %all-gather.8.cloned.1.call-done), kind=kOutput, calls=%fused_computation.39 | convolution fusion | flops 8589934592 | bytes 20971520 | tf_op jit(solution)/shard_map/td,edf->etf/dot_general | solution.py:72
  233.6 3.1 multiply_convert_fusion
  237.8 25.4 %collective-permute-done = bf16[2,2048,256]{1,2,0:T(8,128)(2,1)S(1)} collective-permute-done((bf16[2,2048,256]{1,2,0:T(8,128)(2,1)}, bf16[2,2048,256]{1,2,0:T(8,128)(2,1)S(1)}, u32[]{:S(2)}, u32[]{:S(2)}) %collective-permute-start) | collective-permute-done | bytes 2097184 | tf_op jit(solution)/shard_map/ppermute | solution.py:81
  264.9 45.5 %collective-permute-done.1 = bf16[2,2048,256]{1,2,0:T(8,128)(2,1)} collective-permute-done((bf16[2,2048,256]{1,2,0:T(8,128)(2,1)S(1)}, bf16[2,2048,256]{1,2,0:T(8,128)(2,1)}, u32[]{:S(2)}, u32[]{:S(2)}) %collective-permute-start.1) | collective-permute-done | bytes 2097184 | tf_op jit(solution)/shard_map/ppermute | solution.py:81
  312.3 4.9 %constant_dynamic-update-slice_fusion.5 = bf16[2,2048,2048]{1,2,0:T(8,128)(2,1)S(1)} fusion(bf16[2,2048,2048]{1,2,0:T(8,128)(2,1)S(1)} %constant_dynamic-update-slice_fusion.6, f32[2,2048]{1,0:T(2,128)S(1)} %bitcast.174, f32[2,2048,512]{1,2,0:T(8,128)} %copy-done.2), kind=kLoop, calls=%fused_computation.90 | loop fusion | flops 9437184 | bytes 10502144
  324.6 5.8 %bitcast_convert_fusion = bf16[2048,512]{1,0:T(8,128)(2,1)} fusion(bf16[2,1024,512]{2,1,0:T(8,128)(2,1)S(1)} %copy-done.6, bf16[2,2048,2048]{1,2,0:T(8,128)(2,1)S(1)} %constant_dynamic-update-slice_fusion, s32[]{:T(128)S(6)} %select_n.59), kind=kOutput, calls=%fused_computation.42 | convolution fusion | flops 4296015872 | bytes 12582916 | tf_op jit(solution)/shard_map/etf,efd->td/dot_general | solution.py:89
  330.5 67.7 %reduce-scatter.5.cloned.1.call-done = bf16[256,512]{1,0:T(8,128)(2,1)} async-done(((bf16[2048,512]{1,0:T(8,128)(2,1)}), bf16[256,512]{1,0:T(8,128)(2,1)}) %reduce-scatter.5.cloned.1.call-update) | async-done | bytes 262160 | tf_op jit(solution)/shard_map/reduce_scatter | solution.py:92
  398.2 1.9 multiply_reduce_fusion.2
  400.1 8.8 %copy.115 = bf16[2048,3,512]{0,2,1:T(8,128)(2,1)} copy(bf16[2048,3,512]{2,0,1:T(8,128)(2,1)} %param.33) | data formatting | bytes 12582912 | tf_op args[14]
  408.9 7.1 %all-gather.10.cloned.1.call-done = bf16[256,2048]{1,0:T(8,128)(2,1)} async-done(((bf16[256,512]{1,0:T(8,128)(2,1)}), bf16[256,2048]{1,0:T(8,128)(2,1)}) %all-gather.10.cloned.1.call-update) | async-done | bytes 1048592 | tf_op jit(solution)/shard_map/all_gather | solution.py:231
  416.0 5.1 %fusion.29 = f32[256,3,512]{2,0,1:T(8,128)S(1)} fusion(bf16[2048,3,512]{0,2,1:T(8,128)(2,1)} %copy.115, bf16[256,2048]{1,0:T(8,128)(2,1)} %all-gather.10.cloned.1.call-done), kind=kOutput, calls=%fused_computation.37 | convolution fusion | flops 1610612736 | bytes 8912896 | tf_op jit(solution)/shard_map/dot_general | solution.py:230
  422.4 5.9 %all-reduce = (f32[256]{0:T(256)S(1)}, f32[256]{0:T(256)S(1)}, f32[256]{0:T(256)S(1)}) all-reduce(f32[256]{0:T(256)S(1)} %get-tuple-element.107, f32[256]{0:T(256)S(1)} %get-tuple-element.142, f32[256]{0:T(256)S(1)} %get-tuple-element.106), channel_id=1, replica_groups=mesh['seq'=8,'tp'=4] {'tp'}, use_global_device_ids=true, to_apply=%region_16.17 | all-reduce | flops 768 | bytes 6144 | tf_op jit(solution)/shard_map/psum | solution.py:237
  428.3 2.4 fusion.44
  (131 shorter events, 53.9 us)
Async XLA Ops:
  7.2 66.5 %copy-start = (bf16[512,2048]{1,0:T(8,128)(2,1)S(1)}, bf16[512,2048]{1,0:T(8,128)(2,1)}, u32[]{:S(2)}) copy-start(bf16[512,2048]{1,0:T(8,128)(2,1)} %param.26) | copy-start | bytes 6291460
  7.2 63.4 %all-gather.6.cloned.1.call-start = ((), (), s32[]{:S(2)}) async-start(), calls=%async_computation.2 | async-start | bytes 10485760 | tf_op jit(solution)/shard_map/all_gather | solution.py:167
  7.9 92.5 %reduce-scatter.3.cloned.1.call-start = ((), (), s32[]{:S(2)}) async-start(), calls=%async_computation.3 | async-start | bytes 1310720 | tf_op jit(solution)/shard_map/reduce_scatter | solution.py:210
  9.9 6.4 %copy-start.7 = (bf16[256,512]{1,0:T(8,128)(2,1)S(1)}, bf16[256,512]{1,0:T(8,128)(2,1)}, u32[]{:S(2)}) copy-start(bf16[256,512]{1,0:T(8,128)(2,1)} %param.20) | copy-start | bytes 786436
  56.0 19.4 %copy-start.8 = (f32[256,8]{0,1:T(8,128)S(1)}, f32[256,8]{0,1:T(8,128)}, u32[]{:S(2)}) copy-start(f32[256,8]{0,1:T(8,128)} %param.29) | copy-start | bytes 24580
  56.0 19.4 %copy-start.9 = (s32[256,8]{0,1:T(8,128)S(1)}, s32[256,8]{0,1:T(8,128)}, u32[]{:S(2)}) copy-start(s32[256,8]{0,1:T(8,128)} %param.28) | copy-start | bytes 24580
  56.0 44.4 %copy-start.4 = (bf16[256,512]{1,0:T(8,128)(2,1)S(1)}, bf16[256,512]{1,0:T(8,128)(2,1)}, u32[]{:S(2)}) copy-start(bf16[256,512]{1,0:T(8,128)(2,1)} %param.19) | copy-start | bytes 786436
  56.0 51.2 %copy-start.10 = (f32[512]{0:T(512)S(1)}, f32[512]{0:T(512)}, u32[]{:S(2)}) copy-start(f32[512]{0:T(512)} %param.27) | copy-start | bytes 6148
  75.3 85.7 %all-gather.12.cloned.1.call-start = ((), (), s32[]{:S(2)}) async-start(), calls=%async_computation.7 | async-start | bytes 2506752 | tf_op jit(solution)/shard_map/all_gather | solution.py:64
  109.1 112.0 %all-gather.8.cloned.1.call-start = ((), (), s32[]{:S(2)}) async-start(), calls=%async_computation.4 | async-start | bytes 10485760 | tf_op jit(solution)/shard_map/all_gather | solution.py:70
  164.1 234.1 %reduce-scatter.5.cloned.1.call-start = ((), (), s32[]{:S(2)}) async-start(), calls=%async_computation.5 | async-start | bytes 2359296 | tf_op jit(solution)/shard_map/reduce_scatter | solution.py:92
  233.6 3.9 copy-start.2
  237.5 25.7 %collective-permute-start = (bf16[2,2048,256]{1,2,0:T(8,128)(2,1)}, bf16[2,2048,256]{1,2,0:T(8,128)(2,1)S(1)}, u32[]{:S(2)}, u32[]{:S(2)}) collective-permute-start(bf16[2,2048,256]{1,2,0:T(8,128)(2,1)} %multiply_convert_fusion), channel_id=1, source_target_pairs={{0,1},{1,2},{2,3},{3,0},{4,5},{5,6},{6,7},{7,4},{8,9},{9,10},{10,1... | collective-permute-start | bytes 6291464 | tf_op jit(solution)/shard_map/ppermute | solution.py:81
  263.2 47.2 %collective-permute-start.1 = (bf16[2,2048,256]{1,2,0:T(8,128)(2,1)S(1)}, bf16[2,2048,256]{1,2,0:T(8,128)(2,1)}, u32[]{:S(2)}, u32[]{:S(2)}) collective-permute-start(bf16[2,2048,256]{1,2,0:T(8,128)(2,1)S(1)} %collective-permute-done), channel_id=1, source_target_pairs={{0,1},{1,2},{2,3},{3,0},{4,5},{5,6},{6,7},{7,4},{8,9},{9,10},{10,1... | collective-permute-start | bytes 6291464 | tf_op jit(solution)/shard_map/ppermute | solution.py:81
  263.2 54.0 %collective-permute-start.2 = (bf16[2,2048,256]{1,2,0:T(8,128)(2,1)}, bf16[2,2048,256]{1,2,0:T(8,128)(2,1)}, u32[]{:S(2)}, u32[]{:S(2)}) collective-permute-start(bf16[2,2048,256]{1,2,0:T(8,128)(2,1)} %multiply_convert_fusion), channel_id=1, source_target_pairs={{0,3},{1,0},{2,1},{3,2},{4,7},{5,4},{6,5},{7,6},{8,11},{9,8},{10,9... | collective-permute-start | bytes 6291464 | tf_op jit(solution)/shard_map/ppermute | solution.py:84
  312.3 8.7 %slice-start = ((s8[8388608]{0:T(1024)(128)(4,1)}), s8[4194304]{0:T(1024)(128)(4,1)S(1)}, s32[]{:S(2)}) async-start(s8[8388608]{0:T(1024)(128)(4,1)} %bitcast.163), calls=%async_computation.8 | async-start | bytes 8388608
  317.2 3.8 slice-start.1
  322.4 2.2 copy-start.6
  324.6 73.6 %copy-start.5 = (bf16[256,512]{1,0:T(8,128)(2,1)S(1)}, bf16[256,512]{1,0:T(8,128)(2,1)}, u32[]{:S(2)}) copy-start(bf16[256,512]{1,0:T(8,128)(2,1)} %reduce-scatter.3.cloned.1.call-done) | copy-start | bytes 786436
  324.6 73.6 %copy-start.11 = (f32[512]{0:T(512)S(1)}, f32[512]{0:T(512)}, u32[]{:S(2)}) copy-start(f32[512]{0:T(512)} %param.32) | copy-start | bytes 6148
  330.4 85.5 %all-gather.10.cloned.1.call-start = ((), (), s32[]{:S(2)}) async-start(), calls=%async_computation.6 | async-start | bytes 1310720 | tf_op jit(solution)/shard_map/all_gather | solution.py:231
  408.9 19.4 %copy-start.12 = (f32[512]{0:T(512)S(1)}, f32[512]{0:T(512)}, u32[]{:S(2)}) copy-start(f32[512]{0:T(512)} %param.35) | copy-start | bytes 6148
  408.9 19.4 %copy-start.13 = (f32[512]{0:T(512)S(1)}, f32[512]{0:T(512)}, u32[]{:S(2)}) copy-start(f32[512]{0:T(512)} %param.34) | copy-start | bytes 6148
  416.0 14.7 %copy-start.1 = (bf16[512,2048]{1,0:T(8,128)(2,1)S(1)}, bf16[512,2048]{1,0:T(8,128)(2,1)}, u32[]{:S(2)}) copy-start(bf16[512,2048]{1,0:T(8,128)(2,1)} %param.26) | copy-start | bytes 6291460
  (1 other events, 1.1 us)
Sparse Core Ops, SparseCore 0:
  9.6 60.9 all-gather.5
  75.5 24.8 reduce-scatter.2
  109.2 51.7 all-gather.11
  164.2 56.7 all-gather.7
  330.6 67.5 reduce-scatter.4
  400.2 15.7 all-gather.9
